TPU v7x, 32 devices: a whole 2x2x4 slice. The times are simulated.
32 devices in a mesh: cell: 16 (over z, y, core), bin: 2 (over x).
Axes of the slice: x: 2, y: 2, z: 4, core: 2. Of those that a mesh axis runs over, the one named last changes fastest.
Arguments:
- tensor: float32 [96, 4096, 1024], P('cell', None, 'bin'), may hold values from -6 to 6
- cell_factor: float32 [4096, 128], P('cell'), may hold values from -4 to 4
- bin_factor: float32 [1024, 128], P('bin'), may hold values from -4 to 4
Outputs:
- updated: float32 [96, 128], P('cell', 'bin')
All inputs are finite; a program needn't handle non-finite values.
Results may differ from a plain program's by a relative error of at most 0.000096.
Values sent between devices are 32-bit elements; how exact they have to be, the bound alone decides.
No kernel may reach another device: no remote copies, remote signals or barrier semaphores. Data moves between devices by JAX's collectives and lax.ppermute only.
A program may use at most 128 MiB of HBM per device.

v0:
```python
import jax
import jax.numpy as jnp
from jax import lax
from jax.sharding import PartitionSpec as P


def body(tensor, cell_factor, bin_factor):
    highest = lax.Precision.HIGHEST
    image_rows, cell_count, bin_count = tensor.shape
    rank_cols = bin_factor.shape[1]
    projected = jnp.dot(
        tensor.reshape(image_rows * cell_count, bin_count), bin_factor, precision=highest
    )
    projected = projected.reshape(image_rows, cell_count, rank_cols)
    bin_local = jnp.dot(bin_factor.T, bin_factor, precision=highest)
    gram_bin = lax.psum(bin_local, "bin")
    mttkrp = jnp.sum(
        projected * lax.all_gather(cell_factor, "cell", axis=0, tiled=True)[None, :, :], axis=1
    )
    cell_local = jnp.dot(cell_factor.T, cell_factor, precision=highest)
    gram_cell = lax.psum(cell_local, "cell")
    gram = gram_cell * gram_bin
    chol_lower = jnp.linalg.cholesky(gram)
    totals = lax.psum(mttkrp, "bin")
    solved = jax.scipy.linalg.cho_solve((chol_lower, True), totals.T).T
    own_cols = rank_cols // lax.axis_size("bin")
    updated = lax.dynamic_slice_in_dim(solved, lax.axis_index("bin") * own_cols, own_cols, 1)
    return updated


def solution(mesh):
    placed = (P("cell", None, "bin"), P("cell", None), P("bin", None))
    return jax.shard_map(
        body, mesh=mesh, in_specs=placed, out_specs=P("cell", "bin"), check_vma=False
    )
```

profile of v0, /device:TPU:0, one launch (start us, length us, event | category | flops | bytes accessed | tf_op | source)
XLA Modules:
  0.0 223.3 jit_solution(393272512199881900)
XLA Ops:
  6.5 0.0 copy-start
  6.5 0.0 all-reduce.3.cloned.1.call-start
  6.5 2.0 fusion.7
  8.6 0.0 all-reduce.3.cloned.1.call-update
  8.6 0.0 all-reduce.5.cloned.1.call-start
  8.6 0.0 copy-done
  8.6 1.2 fusion.8
  9.8 0.0 all-reduce.5.cloned.1.call-update
  9.9 0.0 all-gather.2.cloned.1.call-start
  9.9 0.7 all-gather.2.cloned.1.call-update
  10.6 87.4 %all-reduce.3.cloned.1.call-done = f32[128,128]{0,1:T(8,128)} async-done(((f32[128,128]{0,1:T(8,128)}), f32[128,128]{0,1:T(8,128)}) %all-reduce.3.cloned.1.call-update) | async-done | bytes 65552 | tf_op jit(solution)/shard_map/psum | solution.py:21
  98.0 24.7 %all-reduce.5.cloned.1.call-done = f32[128,128]{0,1:T(8,128)} async-done(((f32[128,128]{0,1:T(8,128)}), f32[128,128]{0,1:T(8,128)}) %all-reduce.5.cloned.1.call-update) | async-done | bytes 65552 | tf_op jit(solution)/shard_map/psum | solution.py:16
  122.7 0.9 mul.14
  123.6 0.1 copy.9
  123.7 11.7 %cholesky.16 = f32[128,128]{1,0:T(8,128)S(1)} custom-call(f32[128,128]{1,0:T(8,128)S(1)} %fusion.6), custom_call_target="Cholesky" | custom-call | tf_op jit(solution)/shard_map/jit(cholesky)/cholesky | solution.py:23
  135.5 0.6 compare_reduce_fusion
  136.1 0.7 fusion.1
  136.8 9.8 %custom-call.10 = f32[1,128,128]{1,2,0:T(8,128)S(1)} custom-call(f32[1,128,128]{2,1,0:T(8,128)S(1)} %fusion.1), custom_call_target="InvertDiagBlocksLowerTriangular" | custom-call | tf_op jit(solution)/shard_map/jit(_cho_solve)/triangular_solve | solution.py:25
  146.6 20.2 %all-gather.2.cloned.1.call-done = f32[4096,128]{1,0:T(8,128)} async-done(((f32[256,128]{1,0:T(8,128)}), f32[4096,128]{1,0:T(8,128)}) %all-gather.2.cloned.1.call-update) | async-done | bytes 2097168 | tf_op jit(solution)/shard_map/all_gather | solution.py:18
  166.8 43.8 %multiply_reduce_fusion = f32[6,128]{1,0:T(8,128)S(1)} fusion(f32[6,4096,512]{2,1,0:T(8,128)} %param.3, f32[4096,128]{1,0:T(8,128)} %all-gather.2.cloned.1.call-done, f32[512,128]{1,0:T(8,128)S(1)} %copy-done), kind=kOutput, calls=%fused_computation | convolution fusion | flops 19333644288 | bytes 52694016 | tf_op jit(solution)/shard_map/dot_general | solution.py:11
  210.7 4.9 %psum.23 = f32[6,128]{1,0:T(8,128)S(1)} all-reduce(f32[6,128]{1,0:T(8,128)S(1)} %multiply_reduce_fusion), channel_id=1, replica_groups=mesh['cell'=16,'bin'=2] {'bin'}, use_global_device_ids=true, to_apply=%region_5.6 | all-reduce | flops 768 | bytes 6144 | tf_op jit(solution)/shard_map/psum | solution.py:24
  215.6 0.3 fusion.4
  215.9 0.2 fusion.2
  216.1 0.7 constant_dynamic-slice_fusion
  (2 shorter events, 0.0 us)
Async XLA Ops:
  6.5 2.1 copy-start
  6.5 91.5 %all-reduce.3.cloned.1.call-start = ((), (), s32[]{:S(2)}) async-start(), calls=%async_computation | async-start | bytes 131072 | tf_op jit(solution)/shard_map/psum | solution.py:21
  8.6 114.1 %all-reduce.5.cloned.1.call-start = ((), (), s32[]{:S(2)}) async-start(), calls=%async_computation.1 | async-start | bytes 131072 | tf_op jit(solution)/shard_map/psum | solution.py:16
  9.9 156.9 %all-gather.2.cloned.1.call-start = ((), (), s32[]{:S(2)}) async-start(), calls=%async_computation.2 | async-start | bytes 2228224 | tf_op jit(solution)/shard_map/all_gather | solution.py:18
Sparse Core Ops, SparseCore 0:
  10.8 87.1 all-reduce.2
  100.3 22.3 all-reduce.4
  125.1 41.6 all-gather.1
where the time goes:
time: 224 us; the launch traced here: 223 us
  waiting for transfers between devices  133 us (59%)
  matrix products  47.5 us (21%)
  other arithmetic  23.8 us (11%)
  between operations  13.2 us (6%)
  blocking collectives  4.95 us (2%)
    psum x1, waiting for transfers between devices, body(): gram_cell = lax.psum(cell_local, 'cell')  87.4 us
    dot_general x1, matrix products, body(): jnp.dot(tensor.reshape(image_rows * cell_count, bin_count), bin_factor, p...  43.8 us
    psum x1, waiting for transfers between devices, body(): gram_bin = lax.psum(bin_local, 'bin')  24.7 us
    all_gather x1, waiting for transfers between devices, body(): lax.all_gather(cell_factor, 'cell', axis=0, tiled=True)[None, :, :]  20.2 us
    another operation x3, other arithmetic, body(): chol_lower = jnp.linalg.cholesky(gram)  12.4 us
    another operation x2, other arithmetic, body(): solved = jax.scipy.linalg.cho_solve((chol_lower, True), totals.T).T  10.5 us
    psum x1, blocking collectives, body(): totals = lax.psum(mttkrp, 'bin')  4.95 us
  transfers between devices with their start and end apart: 3, of which 3 were waited for; matrix products, arithmetic and copies ran while one was open for 11% of the time, Pallas kernels for 0%

commit v1 on v0

--- a/solution.py
+++ b/solution.py
@@ -2,6 +2,27 @@
 import jax.numpy as jnp
 from jax import lax
 from jax.sharding import PartitionSpec as P
+
+
+def ring_gather(array, axis, dim):
+    peers, index, rows = (lax.axis_size(axis), lax.axis_index(axis), array.shape[dim])
+    right = [(i, (i + 1) % peers) for i in range(peers)]
+    left = [(i, (i - 1) % peers) for i in range(peers)]
+    out = jnp.zeros((*array.shape[:dim], peers * rows, *array.shape[dim + 1 :]), array.dtype)
+    out = lax.dynamic_update_slice_in_dim(out, array, index * rows, axis=dim)
+    from_left = from_right = array
+    half = peers // 2
+    for step in range(1, half + 1):
+        from_left = lax.ppermute(from_left, axis, right)
+        out = lax.dynamic_update_slice_in_dim(
+            out, from_left, (index - step) % peers * rows, axis=dim
+        )
+        if step < peers - half:
+            from_right = lax.ppermute(from_right, axis, left)
+            out = lax.dynamic_update_slice_in_dim(
+                out, from_right, (index + step) % peers * rows, axis=dim
+            )
+    return out
 
 
 def body(tensor, cell_factor, bin_factor):
@@ -14,9 +35,7 @@
     projected = projected.reshape(image_rows, cell_count, rank_cols)
     bin_local = jnp.dot(bin_factor.T, bin_factor, precision=highest)
     gram_bin = lax.psum(bin_local, "bin")
-    mttkrp = jnp.sum(
-        projected * lax.all_gather(cell_factor, "cell", axis=0, tiled=True)[None, :, :], axis=1
-    )
+    mttkrp = jnp.sum(projected * ring_gather(cell_factor, "cell", 0)[None, :, :], axis=1)
     cell_local = jnp.dot(cell_factor.T, cell_factor, precision=highest)
     gram_cell = lax.psum(cell_local, "cell")
     gram = gram_cell * gram_bin

time: 224 us -> 254 us (1.13)
  starting transfers between devices: 0.09 us -> 32.3 us
  waiting for transfers between devices: 133 us -> 130 us
    ppermute x0 -> x15, starting transfers between devices: none -> 32.2 us  [the longest x7 31.7 us: ring_gather(): from_right = lax.ppermute(from_right, axis, left)]
    ppermute x0 -> x15, waiting for transfers between devices: none -> 23.1 us  [the longest x8 23.1 us: ring_gather(): from_left = lax.ppermute(from_left, axis, right)]
    all_gather x1 -> x0, waiting for transfers between devices: 20.2 us -> none  [body(): lax.all_gather(cell_factor, 'cell', axis=0, tiled=True)[None, :, :]]
    psum x1, waiting for transfers between devices: 87.4 us -> 82.2 us  [body(): gram_cell = lax.psum(cell_local, 'cell')]
  transfers between devices with their start and end apart: 3 -> 17, of which waited for: 3 -> 9; matrix products, arithmetic and copies ran while one was open for 11% -> 11% of each run, Pallas kernels for 0% -> 0%
where the time goes in v1:
time: 254 us; the launch traced here: 253 us
  waiting for transfers between devices  130 us (51%)
  matrix products  47.2 us (19%)
  starting transfers between devices  32.3 us (13%)
  other arithmetic  23.7 us (9%)
  between operations  13.9 us (5%)
  blocking collectives  4.95 us (2%)
    psum x1, waiting for transfers between devices, body(): gram_cell = lax.psum(cell_local, 'cell')  82.2 us
    dot_general x1, matrix products, body(): jnp.dot(tensor.reshape(image_rows * cell_count, bin_count), bin_factor, p...  43.5 us
    ppermute x7, starting transfers between devices, ring_gather(): from_right = lax.ppermute(from_right, axis, left)  31.7 us
    psum x1, waiting for transfers between devices, body(): gram_bin = lax.psum(bin_local, 'bin')  24.7 us
    ppermute x8, waiting for transfers between devices, ring_gather(): from_left = lax.ppermute(from_left, axis, right)  23.1 us
    another operation x3, other arithmetic, body(): chol_lower = jnp.linalg.cholesky(gram)  12.4 us
    another operation x2, other arithmetic, body(): solved = jax.scipy.linalg.cho_solve((chol_lower, True), totals.T).T  10.5 us
  transfers between devices with their start and end apart: 17, of which 9 were waited for; matrix products, arithmetic and copies ran while one was open for 11% of the time, Pallas kernels for 0%

profile of v1, /device:TPU:0, one launch (start us, length us, event | category | flops | bytes accessed | tf_op | source)
XLA Modules:
  0.0 253.3 jit_solution(5246017661414581719)
XLA Ops:
  6.5 0.0 copy-start
  6.5 0.0 copy-start.1
  6.5 0.0 all-reduce.3.cloned.1.call-start
  6.5 0.5 collective-permute-start
  7.0 5.1 %collective-permute-start.1 = (f32[256,128]{1,0:T(8,128)}, f32[256,128]{1,0:T(8,128)S(1)}, u32[]{:S(2)}, u32[]{:S(2)}) collective-permute-start(f32[256,128]{1,0:T(8,128)} %param.4), channel_id=1, source_target_pairs={{0,30},{2,0},{4,2},{6,4},{8,6},{10,8},{12,10},{14,12},{16,14},{18,... | collective-permute-start | bytes 393224 | tf_op jit(solution)/shard_map/ppermute | solution.py:21
  12.0 2.0 fusion.10
  14.0 0.0 all-reduce.3.cloned.1.call-update
  14.1 0.0 all-reduce.5.cloned.1.call-start
  14.1 0.0 copy-done
  14.1 1.2 fusion.11
  15.3 0.0 all-reduce.5.cloned.1.call-update
  15.7 0.1 mul.65
  15.8 0.0 copy-done.1
  15.8 82.2 %all-reduce.3.cloned.1.call-done = f32[128,128]{0,1:T(8,128)} async-done(((f32[128,128]{0,1:T(8,128)}), f32[128,128]{0,1:T(8,128)}) %all-reduce.3.cloned.1.call-update) | async-done | bytes 65552 | tf_op jit(solution)/shard_map/psum | solution.py:40
  98.0 24.7 %all-reduce.5.cloned.1.call-done = f32[128,128]{0,1:T(8,128)} async-done(((f32[128,128]{0,1:T(8,128)}), f32[128,128]{0,1:T(8,128)}) %all-reduce.5.cloned.1.call-update) | async-done | bytes 65552 | tf_op jit(solution)/shard_map/psum | solution.py:37
  122.8 0.9 mul.64
  123.6 0.1 copy.9
  123.8 11.7 %cholesky.16 = f32[128,128]{1,0:T(8,128)S(1)} custom-call(f32[128,128]{1,0:T(8,128)S(1)} %fusion.9), custom_call_target="Cholesky" | custom-call | tf_op jit(solution)/shard_map/jit(cholesky)/cholesky | solution.py:42
  135.5 0.6 compare_reduce_fusion
  136.2 0.7 fusion.4
  136.8 9.8 %custom-call.10 = f32[1,128,128]{1,2,0:T(8,128)S(1)} custom-call(f32[1,128,128]{2,1,0:T(8,128)S(1)} %fusion.4), custom_call_target="InvertDiagBlocksLowerTriangular" | custom-call | tf_op jit(solution)/shard_map/jit(_cho_solve)/triangular_solve | solution.py:44
  146.6 0.0 collective-permute-done
  146.6 0.1 collective-permute-start.2
  146.7 0.0 collective-permute-done.1
  146.7 4.4 %collective-permute-start.3 = (f32[256,128]{1,0:T(8,128)S(1)}, f32[256,128]{1,0:T(8,128)S(1)}, u32[]{:S(2)}, u32[]{:S(2)}) collective-permute-start(f32[256,128]{1,0:T(8,128)S(1)} %collective-permute-done.1), channel_id=1, source_target_pairs={{0,30},{2,0},{4,2},{6,4},{8,6},{10,8},{12,10},{14,12},{16,14},{18,... | collective-permute-start | bytes 393224 | tf_op jit(solution)/shard_map/ppermute | solution.py:21
  151.2 2.7 %collective-permute-done.2 = f32[256,128]{1,0:T(8,128)S(1)} collective-permute-done((f32[256,128]{1,0:T(8,128)S(1)}, f32[256,128]{1,0:T(8,128)S(1)}, u32[]{:S(2)}, u32[]{:S(2)}) %collective-permute-start.2) | collective-permute-done | bytes 131104 | tf_op jit(solution)/shard_map/ppermute | solution.py:16
  153.9 0.0 collective-permute-start.4
  153.9 0.0 collective-permute-done.3
  153.9 4.4 %collective-permute-start.5 = (f32[256,128]{1,0:T(8,128)S(1)}, f32[256,128]{1,0:T(8,128)S(1)}, u32[]{:S(2)}, u32[]{:S(2)}) collective-permute-start(f32[256,128]{1,0:T(8,128)S(1)} %collective-permute-done.3), channel_id=1, source_target_pairs={{0,30},{2,0},{4,2},{6,4},{8,6},{10,8},{12,10},{14,12},{16,14},{18,... | collective-permute-start | bytes 393224 | tf_op jit(solution)/shard_map/ppermute | solution.py:21
  158.4 2.6 %collective-permute-done.4 = f32[256,128]{1,0:T(8,128)S(1)} collective-permute-done((f32[256,128]{1,0:T(8,128)S(1)}, f32[256,128]{1,0:T(8,128)S(1)}, u32[]{:S(2)}, u32[]{:S(2)}) %collective-permute-start.4) | collective-permute-done | bytes 131104 | tf_op jit(solution)/shard_map/ppermute | solution.py:16
  161.0 0.0 collective-permute-start.6
  161.0 0.0 collective-permute-done.5
  161.0 4.4 %collective-permute-start.7 = (f32[256,128]{1,0:T(8,128)S(1)}, f32[256,128]{1,0:T(8,128)S(1)}, u32[]{:S(2)}, u32[]{:S(2)}) collective-permute-start(f32[256,128]{1,0:T(8,128)S(1)} %collective-permute-done.5), channel_id=1, source_target_pairs={{0,30},{2,0},{4,2},{6,4},{8,6},{10,8},{12,10},{14,12},{16,14},{18,... | collective-permute-start | bytes 393224 | tf_op jit(solution)/shard_map/ppermute | solution.py:21
  165.5 2.7 %collective-permute-done.6 = f32[256,128]{1,0:T(8,128)S(1)} collective-permute-done((f32[256,128]{1,0:T(8,128)S(1)}, f32[256,128]{1,0:T(8,128)S(1)}, u32[]{:S(2)}, u32[]{:S(2)}) %collective-permute-start.6) | collective-permute-done | bytes 131104 | tf_op jit(solution)/shard_map/ppermute | solution.py:16
  168.2 0.0 collective-permute-start.8
  168.2 0.0 collective-permute-done.7
  168.2 4.4 %collective-permute-start.9 = (f32[256,128]{1,0:T(8,128)S(1)}, f32[256,128]{1,0:T(8,128)S(1)}, u32[]{:S(2)}, u32[]{:S(2)}) collective-permute-start(f32[256,128]{1,0:T(8,128)S(1)} %collective-permute-done.7), channel_id=1, source_target_pairs={{0,30},{2,0},{4,2},{6,4},{8,6},{10,8},{12,10},{14,12},{16,14},{18,... | collective-permute-start | bytes 393224 | tf_op jit(solution)/shard_map/ppermute | solution.py:21
  172.7 2.7 %collective-permute-done.8 = f32[256,128]{1,0:T(8,128)S(1)} collective-permute-done((f32[256,128]{1,0:T(8,128)S(1)}, f32[256,128]{1,0:T(8,128)S(1)}, u32[]{:S(2)}, u32[]{:S(2)}) %collective-permute-start.8) | collective-permute-done | bytes 131104 | tf_op jit(solution)/shard_map/ppermute | solution.py:16
  175.4 0.0 collective-permute-start.10
  175.4 0.0 collective-permute-done.9
  175.4 4.4 %collective-permute-start.11 = (f32[256,128]{1,0:T(8,128)S(1)}, f32[256,128]{1,0:T(8,128)S(1)}, u32[]{:S(2)}, u32[]{:S(2)}) collective-permute-start(f32[256,128]{1,0:T(8,128)S(1)} %collective-permute-done.9), channel_id=1, source_target_pairs={{0,30},{2,0},{4,2},{6,4},{8,6},{10,8},{12,10},{14,12},{16,14},{18,... | collective-permute-start | bytes 393224 | tf_op jit(solution)/shard_map/ppermute | solution.py:21
  179.9 2.7 %collective-permute-done.10 = f32[256,128]{1,0:T(8,128)S(1)} collective-permute-done((f32[256,128]{1,0:T(8,128)S(1)}, f32[256,128]{1,0:T(8,128)S(1)}, u32[]{:S(2)}, u32[]{:S(2)}) %collective-permute-start.10) | collective-permute-done | bytes 131104 | tf_op jit(solution)/shard_map/ppermute | solution.py:16
  182.6 0.0 collective-permute-start.12
  182.6 0.0 collective-permute-done.11
  182.6 4.4 %collective-permute-start.13 = (f32[256,128]{1,0:T(8,128)S(1)}, f32[256,128]{1,0:T(8,128)S(1)}, u32[]{:S(2)}, u32[]{:S(2)}) collective-permute-start(f32[256,128]{1,0:T(8,128)S(1)} %collective-permute-done.11), channel_id=1, source_target_pairs={{0,30},{2,0},{4,2},{6,4},{8,6},{10,8},{12,10},{14,12},{16,14},{18,... | collective-permute-start | bytes 393224 | tf_op jit(solution)/shard_map/ppermute | solution.py:21
  187.1 2.6 %collective-permute-done.12 = f32[256,128]{1,0:T(8,128)S(1)} collective-permute-done((f32[256,128]{1,0:T(8,128)S(1)}, f32[256,128]{1,0:T(8,128)S(1)}, u32[]{:S(2)}, u32[]{:S(2)}) %collective-permute-start.12) | collective-permute-done | bytes 131104 | tf_op jit(solution)/shard_map/ppermute | solution.py:16
  189.7 0.0 collective-permute-start.14
  189.7 0.0 collective-permute-done.13
  189.7 7.0 %collective-permute-done.14 = f32[256,128]{1,0:T(8,128)S(1)} collective-permute-done((f32[256,128]{1,0:T(8,128)S(1)}, f32[256,128]{1,0:T(8,128)S(1)}, u32[]{:S(2)}, u32[]{:S(2)}) %collective-permute-start.14) | collective-permute-done | bytes 131104 | tf_op jit(solution)/shard_map/ppermute | solution.py:16
  196.8 43.5 %multiply_reduce_fusion = f32[6,128]{1,0:T(8,128)S(1)} fusion(f32[4096,128]{1,0:T(8,128)S(1)} %constant_dynamic-update-slice_fusion, f32[6,4096,512]{2,1,0:T(8,128)} %param.3, f32[512,128]{1,0:T(8,128)S(1)} %copy-done), kind=kOutput, calls=%fused_computation | convolution fusion | flops 19333644288 | bytes 52694016 | tf_op jit(solution)/shard_map/dot_general | solution.py:32
  240.3 4.9 %psum.23 = f32[6,128]{1,0:T(8,128)S(1)} all-reduce(f32[6,128]{1,0:T(8,128)S(1)} %multiply_reduce_fusion), channel_id=1, replica_groups=mesh['cell'=16,'bin'=2] {'bin'}, use_global_device_ids=true, to_apply=%region_5.6 | all-reduce | flops 768 | bytes 6144 | tf_op jit(solution)/shard_map/psum | solution.py:43
  245.2 0.3 fusion.7
  245.5 0.2 fusion.5
  245.7 0.7 constant_dynamic-slice_fusion
  (18 shorter events, 0.3 us)
Async XLA Ops:
  6.5 7.6 %copy-start = (f32[512,128]{1,0:T(8,128)S(1)}, f32[512,128]{1,0:T(8,128)}, u32[]{:S(2)}) copy-start(f32[512,128]{1,0:T(8,128)} %param.5) | copy-start | bytes 786436
  6.5 9.3 %copy-start.1 = (f32[256,128]{1,0:T(8,128)S(1)}, f32[256,128]{1,0:T(8,128)}, u32[]{:S(2)}) copy-start(f32[256,128]{1,0:T(8,128)} %param.4) | copy-start | bytes 393220
  6.5 91.5 %all-reduce.3.cloned.1.call-start = ((), (), s32[]{:S(2)}) async-start(), calls=%async_computation | async-start | bytes 131072 | tf_op jit(solution)/shard_map/psum | solution.py:40
  6.5 140.1 %collective-permute-start = (f32[256,128]{1,0:T(8,128)}, f32[256,128]{1,0:T(8,128)S(1)}, u32[]{:S(2)}, u32[]{:S(2)}) collective-permute-start(f32[256,128]{1,0:T(8,128)} %param.4), channel_id=1, source_target_pairs={{0,2},{2,4},{4,6},{6,8},{8,10},{10,12},{12,14},{14,16},{16,18},{18... | collective-permute-start | bytes 393224 | tf_op jit(solution)/shard_map/ppermute | solution.py:16
  7.0 139.7 %collective-permute-start.1 = (f32[256,128]{1,0:T(8,128)}, f32[256,128]{1,0:T(8,128)S(1)}, u32[]{:S(2)}, u32[]{:S(2)}) collective-permute-start(f32[256,128]{1,0:T(8,128)} %param.4), channel_id=1, source_target_pairs={{0,30},{2,0},{4,2},{6,4},{8,6},{10,8},{12,10},{14,12},{16,14},{18,... | collective-permute-start | bytes 393224 | tf_op jit(solution)/shard_map/ppermute | solution.py:21
  14.1 108.7 %all-reduce.5.cloned.1.call-start = ((), (), s32[]{:S(2)}) async-start(), calls=%async_computation.1 | async-start | bytes 131072 | tf_op jit(solution)/shard_map/psum | solution.py:37
  146.6 7.2 %collective-permute-start.2 = (f32[256,128]{1,0:T(8,128)S(1)}, f32[256,128]{1,0:T(8,128)S(1)}, u32[]{:S(2)}, u32[]{:S(2)}) collective-permute-start(f32[256,128]{1,0:T(8,128)S(1)} %collective-permute-done), channel_id=1, source_target_pairs={{0,2},{2,4},{4,6},{6,8},{8,10},{10,12},{12,14},{14,16},{16,18},{18... | collective-permute-start | bytes 393224 | tf_op jit(solution)/shard_map/ppermute | solution.py:16
  146.7 7.2 %collective-permute-start.3 = (f32[256,128]{1,0:T(8,128)S(1)}, f32[256,128]{1,0:T(8,128)S(1)}, u32[]{:S(2)}, u32[]{:S(2)}) collective-permute-start(f32[256,128]{1,0:T(8,128)S(1)} %collective-permute-done.1), channel_id=1, source_target_pairs={{0,30},{2,0},{4,2},{6,4},{8,6},{10,8},{12,10},{14,12},{16,14},{18,... | collective-permute-start | bytes 393224 | tf_op jit(solution)/shard_map/ppermute | solution.py:21
  153.9 7.1 %collective-permute-start.4 = (f32[256,128]{1,0:T(8,128)S(1)}, f32[256,128]{1,0:T(8,128)S(1)}, u32[]{:S(2)}, u32[]{:S(2)}) collective-permute-start(f32[256,128]{1,0:T(8,128)S(1)} %collective-permute-done.2), channel_id=1, source_target_pairs={{0,2},{2,4},{4,6},{6,8},{8,10},{10,12},{12,14},{14,16},{16,18},{18... | collective-permute-start | bytes 393224 | tf_op jit(solution)/shard_map/ppermute | solution.py:16
  153.9 7.1 %collective-permute-start.5 = (f32[256,128]{1,0:T(8,128)S(1)}, f32[256,128]{1,0:T(8,128)S(1)}, u32[]{:S(2)}, u32[]{:S(2)}) collective-permute-start(f32[256,128]{1,0:T(8,128)S(1)} %collective-permute-done.3), channel_id=1, source_target_pairs={{0,30},{2,0},{4,2},{6,4},{8,6},{10,8},{12,10},{14,12},{16,14},{18,... | collective-permute-start | bytes 393224 | tf_op jit(solution)/shard_map/ppermute | solution.py:21
  161.0 7.2 %collective-permute-start.6 = (f32[256,128]{1,0:T(8,128)S(1)}, f32[256,128]{1,0:T(8,128)S(1)}, u32[]{:S(2)}, u32[]{:S(2)}) collective-permute-start(f32[256,128]{1,0:T(8,128)S(1)} %collective-permute-done.4), channel_id=1, source_target_pairs={{0,2},{2,4},{4,6},{6,8},{8,10},{10,12},{12,14},{14,16},{16,18},{18... | collective-permute-start | bytes 393224 | tf_op jit(solution)/shard_map/ppermute | solution.py:16
  161.0 7.2 %collective-permute-start.7 = (f32[256,128]{1,0:T(8,128)S(1)}, f32[256,128]{1,0:T(8,128)S(1)}, u32[]{:S(2)}, u32[]{:S(2)}) collective-permute-start(f32[256,128]{1,0:T(8,128)S(1)} %collective-permute-done.5), channel_id=1, source_target_pairs={{0,30},{2,0},{4,2},{6,4},{8,6},{10,8},{12,10},{14,12},{16,14},{18,... | collective-permute-start | bytes 393224 | tf_op jit(solution)/shard_map/ppermute | solution.py:21
  168.2 7.2 %collective-permute-start.8 = (f32[256,128]{1,0:T(8,128)S(1)}, f32[256,128]{1,0:T(8,128)S(1)}, u32[]{:S(2)}, u32[]{:S(2)}) collective-permute-start(f32[256,128]{1,0:T(8,128)S(1)} %collective-permute-done.6), channel_id=1, source_target_pairs={{0,2},{2,4},{4,6},{6,8},{8,10},{10,12},{12,14},{14,16},{16,18},{18... | collective-permute-start | bytes 393224 | tf_op jit(solution)/shard_map/ppermute | solution.py:16
  168.2 7.2 %collective-permute-start.9 = (f32[256,128]{1,0:T(8,128)S(1)}, f32[256,128]{1,0:T(8,128)S(1)}, u32[]{:S(2)}, u32[]{:S(2)}) collective-permute-start(f32[256,128]{1,0:T(8,128)S(1)} %collective-permute-done.7), channel_id=1, source_target_pairs={{0,30},{2,0},{4,2},{6,4},{8,6},{10,8},{12,10},{14,12},{16,14},{18,... | collective-permute-start | bytes 393224 | tf_op jit(solution)/shard_map/ppermute | solution.py:21
  175.4 7.2 %collective-permute-start.10 = (f32[256,128]{1,0:T(8,128)S(1)}, f32[256,128]{1,0:T(8,128)S(1)}, u32[]{:S(2)}, u32[]{:S(2)}) collective-permute-start(f32[256,128]{1,0:T(8,128)S(1)} %collective-permute-done.8), channel_id=1, source_target_pairs={{0,2},{2,4},{4,6},{6,8},{8,10},{10,12},{12,14},{14,16},{16,18},{18... | collective-permute-start | bytes 393224 | tf_op jit(solution)/shard_map/ppermute | solution.py:16
  175.4 7.2 %collective-permute-start.11 = (f32[256,128]{1,0:T(8,128)S(1)}, f32[256,128]{1,0:T(8,128)S(1)}, u32[]{:S(2)}, u32[]{:S(2)}) collective-permute-start(f32[256,128]{1,0:T(8,128)S(1)} %collective-permute-done.9), channel_id=1, source_target_pairs={{0,30},{2,0},{4,2},{6,4},{8,6},{10,8},{12,10},{14,12},{16,14},{18,... | collective-permute-start | bytes 393224 | tf_op jit(solution)/shard_map/ppermute | solution.py:21
  182.6 7.1 %collective-permute-start.12 = (f32[256,128]{1,0:T(8,128)S(1)}, f32[256,128]{1,0:T(8,128)S(1)}, u32[]{:S(2)}, u32[]{:S(2)}) collective-permute-start(f32[256,128]{1,0:T(8,128)S(1)} %collective-permute-done.10), channel_id=1, source_target_pairs={{0,2},{2,4},{4,6},{6,8},{8,10},{10,12},{12,14},{14,16},{16,18},{18... | collective-permute-start | bytes 393224 | tf_op jit(solution)/shard_map/ppermute | solution.py:16
  182.6 7.1 %collective-permute-start.13 = (f32[256,128]{1,0:T(8,128)S(1)}, f32[256,128]{1,0:T(8,128)S(1)}, u32[]{:S(2)}, u32[]{:S(2)}) collective-permute-start(f32[256,128]{1,0:T(8,128)S(1)} %collective-permute-done.11), channel_id=1, source_target_pairs={{0,30},{2,0},{4,2},{6,4},{8,6},{10,8},{12,10},{14,12},{16,14},{18,... | collective-permute-start | bytes 393224 | tf_op jit(solution)/shard_map/ppermute | solution.py:21
  189.7 7.1 %collective-permute-start.14 = (f32[256,128]{1,0:T(8,128)S(1)}, f32[256,128]{1,0:T(8,128)S(1)}, u32[]{:S(2)}, u32[]{:S(2)}) collective-permute-start(f32[256,128]{1,0:T(8,128)S(1)} %collective-permute-done.12), channel_id=1, source_target_pairs={{0,2},{2,4},{4,6},{6,8},{8,10},{10,12},{12,14},{14,16},{16,18},{18... | collective-permute-start | bytes 393224 | tf_op jit(solution)/shard_map/ppermute | solution.py:16
Sparse Core Ops, SparseCore 0:
  14.2 83.8 all-reduce.2
  100.4 22.3 all-reduce.4
